TPU v7x, 512 devices: a whole 4x4x16 slice. The times are simulated.
512 devices in a mesh: dp: 4 (over y), expert: 128 (over x, z, core).
Axes of the slice: x: 4, y: 4, z: 16, core: 2. Of those that a mesh axis runs over, the one named last changes fastest.
Arguments:
- tokens: bfloat16 [12288, 2048], P(('dp', 'expert')), may hold values from -6 to 6
- cotangent: bfloat16 [12288, 2048], P(('dp', 'expert')), may hold values from -6 to 6
- routes: int32 [12288, 8], P(('dp', 'expert')), may hold values from 0 to 127, all different within a row; in each aligned block of 24 rows (0 to 23, 24 to 47, ...) at most 2 rows name the same one
- gates: bfloat16 [12288, 8], P(('dp', 'expert')), may hold values from 0.029907227 to 0.25
- plan: int32 [128], replicated, may hold values from 0 to 127, as said below
- gate_values: bfloat16 [128, 768, 2048], P('expert', 'dp'), may hold values from -0.125 to 0.125
- up_values: bfloat16 [128, 768, 2048], P('expert', 'dp'), may hold values from -0.125 to 0.125
- down_values: bfloat16 [128, 768, 2048], P('expert', 'dp'), may hold values from -0.21875 to 0.21875
- gate_scales: float32 [128, 12, 16], P('expert', 'dp'), may hold values from 0.5 to 2
- up_scales: float32 [128, 12, 16], P('expert', 'dp'), may hold values from 0.5 to 2
- down_scales: float32 [128, 12, 16], P('expert', 'dp'), may hold values from 0.5 to 2
Outputs:
- token_grads: bfloat16 [12288, 2048], P(('dp', 'expert'))
- gate_grads: bfloat16 [128, 768, 2048], P('expert', 'dp')
- up_grads: bfloat16 [128, 768, 2048], P('expert', 'dp')
- down_grads: bfloat16 [128, 768, 2048], P('expert', 'dp')
Inputs may be any that keep to these rules, and one draw needn't show every extreme that they name: `routes`: each token names 8 different experts. Among the 24 tokens of one device no expert is named more than 2 times, and in every draw the tokens of some device name some expert exactly 2 times. plan[plan[s]] = s, and plan[s] is either s or (s + 64) % 128; plan[0] = 64.
All inputs are finite; a program needn't handle non-finite values.
Results may differ from a plain program's by a relative error of at most 0.0082.
Values may be sent and summed in bfloat16 or wider, within the bound.
No kernel may reach another device: no remote copies, remote signals or barrier semaphores. Data moves between devices by JAX's collectives and lax.ppermute only.
A program may use at most 128 MiB of HBM per device.

v0:
```python
import jax
import jax.numpy as jnp
from jax import lax
from jax.sharding import PartitionSpec as P


def swapped(block, axis, stride):
    count = lax.axis_size(axis)
    route = []
    for low in range(count):
        high = low | 1 << stride
        if high != low and high < count:
            route += [(low, high), (high, low)]
    return lax.ppermute(block, axis, route)


def dequantize(values, scales):
    row_block = values.shape[0] // scales.shape[0]
    col_block = values.shape[1] // scales.shape[1]
    spread = jnp.repeat(jnp.repeat(scales, row_block, axis=0), col_block, axis=1)
    return (values.astype(jnp.float32) * spread).astype(jnp.bfloat16)


def slot_choice(route_lists, experts, capacity):
    numbers = jnp.arange(experts, dtype=jnp.int32)
    flattened = route_lists.reshape(-1)
    marked = (flattened[:, None] == numbers).astype(jnp.int32)
    slot_index = jnp.sum((jnp.cumsum(marked, axis=0) - 1) * marked, axis=-1)
    position = flattened * capacity + slot_index
    selected = position[:, None] == jnp.arange(experts * capacity, dtype=jnp.int32)
    return selected.reshape(route_lists.shape + (experts * capacity,))


def contract(left, right, left_dim, right_dim):
    return lax.dot_general(
        left, right, (((left_dim,), (right_dim,)), ((), ())), preferred_element_type=jnp.float32
    )


def expert_work(token_rows, cot_rows, w_gate, w_up, w_down):
    pre_gate = contract(token_rows, w_gate, 1, 1)
    pre_up = contract(token_rows, w_up, 1, 1)
    sigmoid_gate = jax.nn.sigmoid(pre_gate)
    activated = pre_gate * sigmoid_gate
    hidden = (activated * pre_up).astype(jnp.bfloat16)
    grad_hidden = contract(cot_rows, w_down, 1, 1)
    grad_gate = (
        grad_hidden * pre_up * sigmoid_gate * (1.0 + pre_gate * (1.0 - sigmoid_gate))
    ).astype(jnp.bfloat16)
    grad_up = (grad_hidden * activated).astype(jnp.bfloat16)
    gate_grad = contract(grad_gate, token_rows, 0, 0).astype(jnp.bfloat16)
    up_grad = contract(grad_up, token_rows, 0, 0).astype(jnp.bfloat16)
    down_grad = contract(hidden, cot_rows, 0, 0).astype(jnp.bfloat16)
    row_grads = (
        jnp.dot(grad_gate, w_gate, preferred_element_type=jnp.float32)
        + jnp.dot(grad_up, w_up, preferred_element_type=jnp.float32)
    ).astype(jnp.bfloat16)
    return (row_grads, gate_grad, up_grad, down_grad)


def on_device(
    tokens,
    cotangent,
    routes,
    gates,
    plan,
    gate_values,
    up_values,
    down_values,
    gate_scales,
    up_scales,
    down_scales,
):
    tok_count, features = tokens.shape
    experts = lax.axis_size("expert")
    replicas = lax.axis_size("dp")
    capacity = 2
    half_bit = experts.bit_length() - 2
    expert_index = lax.axis_index("expert")
    numbers = jnp.arange(experts, dtype=jnp.int32)
    is_moved = jnp.sum(jnp.where(numbers == expert_index, plan, 0)) != expert_index
    w_gate = dequantize(gate_values[0], gate_scales[0])
    w_up = dequantize(up_values[0], up_scales[0])
    w_down = dequantize(down_values[0], down_scales[0])
    selected = slot_choice(routes, experts, capacity)
    dispatch = (
        jnp.sum(selected.astype(jnp.int32), axis=1)
        .reshape(tok_count, experts, capacity)
        .astype(jnp.bfloat16)
    )
    outgoing = jnp.einsum(
        "rec,rd->ecd", dispatch, tokens, preferred_element_type=jnp.float32
    ).astype(jnp.bfloat16)
    slot_gate = jnp.einsum(
        "rkx,rk->x", selected.astype(jnp.float32), gates.astype(jnp.float32)
    ).reshape(experts, capacity)
    lifted = jnp.einsum("rec,rd->ecd", dispatch, cotangent, preferred_element_type=jnp.float32)
    cot_out = (lifted * slot_gate[..., None]).astype(jnp.bfloat16)
    both = jnp.stack([outgoing, cot_out], axis=0)
    arrived = lax.all_to_all(both, "expert", split_axis=1, concat_axis=1, tiled=True)
    gathered = lax.all_gather(arrived, "dp", axis=1, tiled=True)
    token_rows = gathered[0].reshape(-1, features)
    cot_rows = gathered[1].reshape(-1, features)
    row_grads, gate_grad, up_grad, down_grad = expert_work(
        token_rows, cot_rows, w_gate, w_up, w_down
    )
    summed_rows = lax.psum_scatter(
        row_grads.reshape(replicas, experts, capacity, features),
        "dp",
        scatter_dimension=0,
        tiled=True,
    )
    returned = lax.all_to_all(summed_rows[0], "expert", split_axis=0, concat_axis=0, tiled=True)
    token_grads = jnp.einsum(
        "rec,ecd->rd", dispatch, returned, preferred_element_type=jnp.float32
    ).astype(jnp.bfloat16)
    arrived_grads = swapped((gate_grad, up_grad, down_grad), "expert", half_bit)
    gate_grad = jnp.where(is_moved, arrived_grads[0], gate_grad)
    up_grad = jnp.where(is_moved, arrived_grads[1], up_grad)
    down_grad = jnp.where(is_moved, arrived_grads[2], down_grad)
    return (token_grads, gate_grad[None], up_grad[None], down_grad[None])


def solution(mesh):
    return jax.shard_map(
        on_device,
        mesh=mesh,
        in_specs=(
            P(("dp", "expert"), None),
            P(("dp", "expert"), None),
            P(("dp", "expert"), None),
            P(("dp", "expert"), None),
            P(),
            P("expert", "dp", None),
            P("expert", "dp", None),
            P("expert", "dp", None),
            P("expert", "dp", None),
            P("expert", "dp", None),
            P("expert", "dp", None),
        ),
        out_specs=(
            P(("dp", "expert"), None),
            P("expert", "dp", None),
            P("expert", "dp", None),
            P("expert", "dp", None),
        ),
        check_vma=False,
    )
```

profile of v0, /device:TPU:1, one launch (start us, length us, event | category | flops | bytes accessed | tf_op | source)
XLA Modules:
  0.0 426.3 jit_solution(17713711811344199833)
XLA Ops:
  7.3 0.8 copy.50
  8.0 0.1 eq.62
  8.1 0.1 iota_compare_fusion.1
  8.3 0.1 fusion.26
  8.5 0.2 fusion.29
  8.7 0.1 reduce_sum.30
  8.8 0.1 convert_reduce_fusion
  8.9 0.1 copy.54
  9.1 0.1 copy.61
  9.1 0.1 copy.57
  9.2 0.7 bitcast_convert_fusion
  9.9 0.7 select_reduce_fusion
  10.6 0.1 copy.69
  10.7 0.5 fusion.2
  11.2 0.5 fusion.1
  11.6 0.2 pad_maximum_fusion
  11.9 2.2 copy.58
  14.0 119.5 %all_to_all.10 = bf16[2,128,2,2048]{3,2,0,1:T(2,128)(2,1)} all-to-all(bf16[2,128,2,2048]{3,2,0,1:T(2,128)(2,1)S(1)} %copy.58), channel_id=1, replica_groups=mesh['dp'=4,'expert'=128] {'expert'}, dimensions={1} | all-to-all | bytes 4194304 | tf_op jit(solution)/shard_map/all_to_all | solution.py:100
  133.5 0.0 reduce-scatter.2.cloned.1.call-start
  133.6 0.6 copy-done.9
  134.2 0.5 copy-done.4
  134.7 0.2 convert_bitcast_fusion.1
  134.9 0.3 copy.78
  135.2 0.4 copy-done.10
  135.5 0.5 copy-done.5
  136.0 0.2 convert_bitcast_fusion.3
  136.2 0.3 copy.76
  136.5 0.8 copy-done.6
  137.3 0.2 convert_bitcast_fusion.4
  137.5 0.3 copy.74
  137.8 0.4 copy-done.11
  138.2 0.5 fusion.8
  138.7 1.4 fusion.9
  140.1 0.5 fusion.10
  140.6 77.3 %all-gather.2.cloned.1.call-done = bf16[2,512,2,2048]{3,2,0,1:T(2,128)(2,1)} async-done(((bf16[2,128,2,2048]{3,2,0,1:T(2,128)(2,1)}), bf16[2,512,2,2048]{3,2,0,1:T(2,128)(2,1)}) %all-gather.2.cloned.1.call-update) | async-done | bytes 8388624 | tf_op jit(solution)/shard_map/all_gather | solution.py:101
  217.9 8.4 %fusion.34 = (bf16[1,512,2,2048]{3,2,0,1:T(2,128)(2,1)}, bf16[1,512,2,2048]{3,2,0,1:T(2,128)(2,1)}) fusion(bf16[2,512,2,2048]{3,2,0,1:T(2,128)(2,1)} %all-gather.2.cloned.1.call-done), kind=kLoop, calls=%fused_computation.70 | loop fusion | bytes 16777216 | tf_op jit(solution)/shard_map/slice | solution.py:103
  226.3 7.2 %reshape_squeeze.7 = bf16[1024,2048]{1,0:T(8,128)(2,1)} reshape(bf16[1,512,2,2048]{3,2,0,1:T(2,128)(2,1)} %get-tuple-element.5) | data formatting | bytes 8388608 | tf_op jit(solution)/shard_map/reshape;squeeze | solution.py:102
  233.5 4.8 %fusion.15 = f32[1024,192]{0,1:T(8,128)} fusion(bf16[1024,2048]{1,0:T(8,128)(2,1)} %reshape_squeeze.7, bf16[24,8,16,128]{3,2,1,0:T(8,128)(2,1)S(1)} %bitcast.130), kind=kOutput, calls=%fused_computation.30 | convolution fusion | flops 805306368 | bytes 5767168 | tf_op jit(solution)/shard_map/dot_general | solution.py:35
  238.2 2.4 fusion.18
  240.7 7.2 %reshape_squeeze.6 = bf16[1024,2048]{1,0:T(8,128)(2,1)} reshape(bf16[1,512,2,2048]{3,2,0,1:T(2,128)(2,1)} %get-tuple-element.4) | data formatting | bytes 8388608 | tf_op jit(solution)/shard_map/reshape;squeeze | solution.py:103
  247.9 4.3 %multiply_convert_fusion.1 = (bf16[1024,192]{0,1:T(8,128)(2,1)S(1)}, bf16[1024,192]{0,1:T(8,128)(2,1)S(1)}) fusion(f32[1024,192]{0,1:T(8,128)} %fusion.15, f32[1024,192]{0,1:T(8,128)} %fusion.18, bf16[1024,2048]{1,0:T(8,128)(2,1)} %reshape_squeeze.6, bf16[24,8,16,128]{3,2,1,0:T(8,128)(2,1)S(1)} %bitcast.129), kind=kOutput, calls=%fused_computation.43 | convolution fusion | flops 807862272 | bytes 7340032 | tf_op jit(solution)/shard_map/dot_general | solution.py:35
  252.2 0.5 broadcast_in_dim.39
  252.7 1.4 fusion.12
  254.1 0.5 broadcast_in_dim.37
  254.5 3.4 add_convert_fusion
  258.0 7.7 %reshape.126 = bf16[4,128,2,2048]{3,2,1,0:T(2,128)(2,1)} reshape(bf16[1024,2048]{1,0:T(8,128)(2,1)} %add_convert_fusion) | data formatting | bytes 8388608 | tf_op jit(solution)/shard_map/reshape | solution.py:108
  265.6 6.0 %copy.59 = bf16[4,128,2,2048]{3,1,2,0:T(8,128)(2,1)} copy(bf16[4,128,2,2048]{3,2,1,0:T(2,128)(2,1)} %reshape.126) | data formatting | bytes 8388608 | tf_op jit(solution)/shard_map/reshape | solution.py:108
  271.7 55.8 %reduce-scatter.2.cloned.1.call-done = bf16[1,128,2,2048]{3,1,2,0:T(8,128)(2,1)} async-done(((bf16[4,128,2,2048]{3,1,2,0:T(8,128)(2,1)}), bf16[1,128,2,2048]{3,1,2,0:T(8,128)(2,1)}) %reduce-scatter.2.cloned.1.call-update) | async-done | bytes 1048592 | tf_op jit(solution)/shard_map/reduce_scatter | solution.py:107
  327.5 3.3 copy.60
  330.8 16.9 %all-to-all-start.1 = ((bf16[128,2,2048]{2,1,0:T(2,128)(2,1)}), bf16[128,2,2048]{2,1,0:T(2,128)(2,1)S(1)}, u32[]{:S(2)}, u32[]{:S(2)}) async-start(bf16[128,2,2048]{2,1,0:T(2,128)(2,1)} %copy.60), calls=%async_computation.2 | async-start | bytes 2097152 | tf_op jit(solution)/shard_map/all_to_all | solution.py:113
  347.7 3.7 convolution_convert_fusion.1
  351.4 5.1 %collective-permute-start.2 = (bf16[192,2048]{1,0:T(8,128)(2,1)S(1)}, bf16[192,2048]{1,0:T(8,128)(2,1)}, u32[]{:S(2)}, u32[]{:S(2)}) collective-permute-start(bf16[192,2048]{1,0:T(8,128)(2,1)S(1)} %convolution_convert_fusion.1), channel_id=1, source_target_pairs={{0,64},{64,0},{1,65},{65,1},{2,66},{66,2},{3,67},{67,3},{4,68},{68... | collective-permute-start | bytes 2359304 | tf_op jit(solution)/shard_map/ppermute | solution.py:14
  356.5 0.6 fusion.32
  357.8 3.3 convolution_convert_fusion.2
  361.2 1.9 collective-permute-start.1
  363.1 1.0 convolution_convert_fusion.3
  364.1 4.9 %collective-permute-start = (bf16[192,2048]{1,0:T(8,128)(2,1)S(1)}, bf16[192,2048]{1,0:T(8,128)(2,1)S(1)}, u32[]{:S(2)}, u32[]{:S(2)}) collective-permute-start(bf16[192,2048]{1,0:T(8,128)(2,1)S(1)} %convolution_convert_fusion.3), channel_id=1, source_target_pairs={{0,64},{64,0},{1,65},{65,1},{2,66},{66,2},{3,67},{67,3},{4,68},{68... | collective-permute-start | bytes 2359304 | tf_op jit(solution)/shard_map/ppermute | solution.py:14
  369.0 9.6 %collective-permute-done.2 = bf16[192,2048]{1,0:T(8,128)(2,1)} collective-permute-done((bf16[192,2048]{1,0:T(8,128)(2,1)S(1)}, bf16[192,2048]{1,0:T(8,128)(2,1)}, u32[]{:S(2)}, u32[]{:S(2)}) %collective-permute-start.2) | collective-permute-done | bytes 786464 | tf_op jit(solution)/shard_map/ppermute | solution.py:14
  378.6 1.0 select_bitcast_fusion
  379.6 20.6 %collective-permute-done.1 = bf16[192,2048]{1,0:T(8,128)(2,1)S(1)} collective-permute-done((bf16[192,2048]{1,0:T(8,128)(2,1)S(1)}, bf16[192,2048]{1,0:T(8,128)(2,1)S(1)}, u32[]{:S(2)}, u32[]{:S(2)}) %collective-permute-start.1) | collective-permute-done | bytes 786464 | tf_op jit(solution)/shard_map/ppermute | solution.py:14
  400.2 1.0 select_bitcast_fusion.1
  401.1 16.1 %collective-permute-done = bf16[192,2048]{1,0:T(8,128)(2,1)S(1)} collective-permute-done((bf16[192,2048]{1,0:T(8,128)(2,1)S(1)}, bf16[192,2048]{1,0:T(8,128)(2,1)S(1)}, u32[]{:S(2)}, u32[]{:S(2)}) %collective-permute-start) | collective-permute-done | bytes 786464 | tf_op jit(solution)/shard_map/ppermute | solution.py:14
  417.2 1.0 select_bitcast_fusion.2
  418.2 1.3 fusion.3
  (40 shorter events, 0.3 us)
Async XLA Ops:
  7.2 3.5 copy-start
  7.2 4.0 copy-start.8
  7.2 210.7 %all-gather.2.cloned.1.call-start = ((), (), s32[]{:S(2)}) async-start(), calls=%async_computation.3 | async-start | bytes 10485760 | tf_op jit(solution)/shard_map/all_gather | solution.py:101
  133.5 0.7 copy-start.9
  133.5 1.1 copy-start.4
  133.5 193.9 %reduce-scatter.2.cloned.1.call-start = ((), (), s32[]{:S(2)}) async-start(), calls=%async_computation.4 | async-start | bytes 5242880 | tf_op jit(solution)/shard_map/reduce_scatter | solution.py:107
  134.8 0.7 copy-start.10
  134.9 1.1 copy-start.5
  136.2 1.1 copy-start.6
  137.5 0.7 copy-start.11
  233.5 4.8 %copy-start.2 = (bf16[1024,2048]{1,0:T(8,128)(2,1)S(1)}, bf16[1024,2048]{1,0:T(8,128)(2,1)}, u32[]{:S(2)}) copy-start(bf16[1024,2048]{1,0:T(8,128)(2,1)} %reshape_squeeze.7) | copy-start | bytes 12582916
  233.5 4.8 %copy-start.7 = (bf16[192,16,128]{2,1,0:T(8,128)(2,1)S(1)}, bf16[192,16,128]{2,1,0:T(8,128)(2,1)}, u32[]{:S(2)}) copy-start(bf16[192,16,128]{2,1,0:T(8,128)(2,1)} %fusion.9) | copy-start | bytes 2359300
  330.8 87.4 %all-to-all-start.1 = ((bf16[128,2,2048]{2,1,0:T(2,128)(2,1)}), bf16[128,2,2048]{2,1,0:T(2,128)(2,1)S(1)}, u32[]{:S(2)}, u32[]{:S(2)}) async-start(bf16[128,2,2048]{2,1,0:T(2,128)(2,1)} %copy.60), calls=%async_computation.2 | async-start | bytes 2097152 | tf_op jit(solution)/shard_map/all_to_all | solution.py:113
  347.7 8.8 %copy-start.12 = (s32[128]{0:T(128)S(1)}, s32[128]{0:T(128)}, u32[]{:S(2)}) copy-start(s32[128]{0:T(128)} %param.15) | copy-start | bytes 1540
  351.4 27.2 %collective-permute-start.2 = (bf16[192,2048]{1,0:T(8,128)(2,1)S(1)}, bf16[192,2048]{1,0:T(8,128)(2,1)}, u32[]{:S(2)}, u32[]{:S(2)}) collective-permute-start(bf16[192,2048]{1,0:T(8,128)(2,1)S(1)} %convolution_convert_fusion.1), channel_id=1, source_target_pairs={{0,64},{64,0},{1,65},{65,1},{2,66},{66,2},{3,67},{67,3},{4,68},{68... | collective-permute-start | bytes 2359304 | tf_op jit(solution)/shard_map/ppermute | solution.py:14
  357.8 5.3 %copy-start.3 = (bf16[1024,2048]{1,0:T(8,128)(2,1)S(1)}, bf16[1024,2048]{1,0:T(8,128)(2,1)}, u32[]{:S(2)}) copy-start(bf16[1024,2048]{1,0:T(8,128)(2,1)} %reshape_squeeze.7) | copy-start | bytes 12582916
  361.2 39.0 %collective-permute-start.1 = (bf16[192,2048]{1,0:T(8,128)(2,1)S(1)}, bf16[192,2048]{1,0:T(8,128)(2,1)S(1)}, u32[]{:S(2)}, u32[]{:S(2)}) collective-permute-start(bf16[192,2048]{1,0:T(8,128)(2,1)S(1)} %convolution_convert_fusion.2), channel_id=1, source_target_pairs={{0,64},{64,0},{1,65},{65,1},{2,66},{66,2},{3,67},{67,3},{4,68},{68... | collective-permute-start | bytes 2359304 | tf_op jit(solution)/shard_map/ppermute | solution.py:14
  364.1 53.1 %collective-permute-start = (bf16[192,2048]{1,0:T(8,128)(2,1)S(1)}, bf16[192,2048]{1,0:T(8,128)(2,1)S(1)}, u32[]{:S(2)}, u32[]{:S(2)}) collective-permute-start(bf16[192,2048]{1,0:T(8,128)(2,1)S(1)} %convolution_convert_fusion.3), channel_id=1, source_target_pairs={{0,64},{64,0},{1,65},{65,1},{2,66},{66,2},{3,67},{67,3},{4,68},{68... | collective-permute-start | bytes 2359304 | tf_op jit(solution)/shard_map/ppermute | solution.py:14
  400.2 19.3 %copy-start.1 = (bf16[24,2048]{1,0:T(8,128)(2,1)S(1)}, bf16[24,2048]{1,0:T(8,128)(2,1)}, u32[]{:S(2)}) copy-start(bf16[24,2048]{1,0:T(8,128)(2,1)} %param.11) | copy-start | bytes 294916
Sparse Core Ops, SparseCore 0:
  133.7 84.1 all-gather.1
  271.8 55.6 reduce-scatter.1
where the time goes:
time: 427 us; the launch traced here: 426 us
  waiting for transfers between devices  179 us (42%)
  blocking collectives  119 us (28%)
  local copies, waits for them, and re-layouts  48.3 us (11%)
  starting transfers between devices  28.9 us (7%)
  matrix products  26.6 us (6%)
  between operations  15 us (4%)
  other arithmetic  8.66 us (2%)
    all_to_all x1, blocking collectives, on_device(): lax.all_to_all(both, 'expert', split_axis=1, concat_axis=1, tiled=True)  119 us
    all_gather x1, waiting for transfers between devices, on_device(): gathered = lax.all_gather(arrived, 'dp', axis=1, tiled=True)  77.3 us
    reduce_scatter x1, waiting for transfers between devices, on_device(): lax.psum_scatter(row_grads.reshape(replicas, experts, capacity, features)...  55.8 us
    ppermute x3, waiting for transfers between devices, swapped(): return lax.ppermute(block, axis, route)  46.3 us
    dot_general x6, matrix products, contract(): lax.dot_general(left, right, (((left_dim,), (right_dim,)), ((), ())), pre...  19.5 us
    all_to_all x1, starting transfers between devices, on_device(): lax.all_to_all(summed_rows[0], 'expert', split_axis=0, concat_axis=0, til...  16.9 us
    reshape x2, local copies, waits for them, and re-layouts, on_device(): row_grads.reshape(replicas, experts, capacity, features)  13.7 us
    ppermute x3, starting transfers between devices, swapped(): return lax.ppermute(block, axis, route)  11.9 us
  transfers between devices with their start and end apart: 6, of which 5 were waited for; matrix products, arithmetic and copies ran while one was open for 4% of the time, Pallas kernels for 0%

commit v1 on v0

--- a/solution.py
+++ b/solution.py
@@ -2,6 +2,27 @@
 import jax.numpy as jnp
 from jax import lax
 from jax.sharding import PartitionSpec as P
+
+
+def gather_around(x, axis, dim):
+    size, index, rows = (lax.axis_size(axis), lax.axis_index(axis), x.shape[dim])
+    upward = [(i, (i + 1) % size) for i in range(size)]
+    backward = [(i, (i - 1) % size) for i in range(size)]
+    result = jnp.zeros((*x.shape[:dim], size * rows, *x.shape[dim + 1 :]), x.dtype)
+    result = lax.dynamic_update_slice_in_dim(result, x, index * rows, axis=dim)
+    from_left = from_right = x
+    half = size // 2
+    for turn in range(1, half + 1):
+        from_left = lax.ppermute(from_left, axis, upward)
+        result = lax.dynamic_update_slice_in_dim(
+            result, from_left, (index - turn) % size * rows, axis=dim
+        )
+        if turn < size - half:
+            from_right = lax.ppermute(from_right, axis, backward)
+            result = lax.dynamic_update_slice_in_dim(
+                result, from_right, (index + turn) % size * rows, axis=dim
+            )
+    return result
 
 
 def swapped(block, axis, stride):
@@ -98,7 +119,7 @@
     cot_out = (lifted * slot_gate[..., None]).astype(jnp.bfloat16)
     both = jnp.stack([outgoing, cot_out], axis=0)
     arrived = lax.all_to_all(both, "expert", split_axis=1, concat_axis=1, tiled=True)
-    gathered = lax.all_gather(arrived, "dp", axis=1, tiled=True)
+    gathered = gather_around(arrived, "dp", 1)
     token_rows = gathered[0].reshape(-1, features)
     cot_rows = gathered[1].reshape(-1, features)
     row_grads, gate_grad, up_grad, down_grad = expert_work(

time: 427 us -> 436 us (1.021)
  waiting for transfers between devices: 179 us -> 160 us
  local copies, waits for them, and re-layouts: 48.3 us -> 63 us
  starting transfers between devices: 28.9 us -> 37.5 us
    all_gather x1 -> x0, waiting for transfers between devices: 77.3 us -> none  [on_device(): gathered = lax.all_gather(arrived, 'dp', axis=1, tiled=True)]
    ppermute x0 -> x3, waiting for transfers between devices: none -> 67 us  [the longest x2 67 us: gather_around(): from_left = lax.ppermute(from_left, axis, upward)]
    dynamic_update_slice x0 -> x4, local copies, waits for them, and re-layouts: none -> 11.1 us  [the longest x2 6.33 us: gather_around(): lax.dynamic_update_slice_in_dim(result, from_left, (index - turn) % size...]
    reduce_scatter x1, waiting for transfers between devices: 55.8 us -> 46.9 us  [on_device(): lax.psum_scatter(row_grads.reshape(replicas, experts, capacity, features)...]
    ppermute x0 -> x3, starting transfers between devices: none -> 8.63 us  [the longest x2 5.28 us: gather_around(): from_left = lax.ppermute(from_left, axis, upward)]
    broadcast_in_dim x0 -> x1, local copies, waits for them, and re-layouts: none -> 4.55 us  [gather_around(): jnp.zeros((*x.shape[:dim], size * rows, *x.shape[dim + 1:]), x.dtype)]
  transfers between devices with their start and end apart: 6 -> 8, of which waited for: 5 -> 6; matrix products, arithmetic and copies ran while one was open for 4% -> 8% of each run, Pallas kernels for 0% -> 0%
where the time goes in v1:
time: 436 us; the launch traced here: 434 us
  waiting for transfers between devices  160 us (37%)
  blocking collectives  119 us (27%)
  local copies, waits for them, and re-layouts  63 us (14%)
  starting transfers between devices  37.5 us (9%)
  matrix products  26.3 us (6%)
  between operations  15.2 us (3%)
  other arithmetic  13 us (3%)
    all_to_all x1, blocking collectives, on_device(): lax.all_to_all(both, 'expert', split_axis=1, concat_axis=1, tiled=True)  119 us
    ppermute x2, waiting for transfers between devices, gather_around(): from_left = lax.ppermute(from_left, axis, upward)  67 us
    reduce_scatter x1, waiting for transfers between devices, on_device(): lax.psum_scatter(row_grads.reshape(replicas, experts, capacity, features)...  46.9 us
    ppermute x3, waiting for transfers between devices, swapped(): return lax.ppermute(block, axis, route)  46 us
    dot_general x6, matrix products, contract(): lax.dot_general(left, right, (((left_dim,), (right_dim,)), ((), ())), pre...  19.3 us
    all_to_all x1, starting transfers between devices, on_device(): lax.all_to_all(summed_rows[0], 'expert', split_axis=0, concat_axis=0, til...  16.7 us
    reshape x2, local copies, waits for them, and re-layouts, on_device(): row_grads.reshape(replicas, experts, capacity, features)  13.7 us
    ppermute x3, starting transfers between devices, swapped(): return lax.ppermute(block, axis, route)  12.1 us
  transfers between devices with their start and end apart: 8, of which 6 were waited for; matrix products, arithmetic and copies ran while one was open for 8% of the time, Pallas kernels for 0%

profile of v1, /device:TPU:1, one launch (start us, length us, event | category | flops | bytes accessed | tf_op | source)
XLA Modules:
  0.0 434.4 jit_solution(13004930689010655251)
XLA Ops:
  7.3 0.8 copy.60
  8.0 0.1 eq.66
  8.1 0.1 iota_compare_fusion.1
  8.3 0.1 fusion.26
  8.5 0.2 fusion.29
  8.7 0.1 reduce_sum.30
  8.8 0.1 convert_reduce_fusion
  8.9 0.1 copy.64
  9.2 0.7 bitcast_convert_fusion
  9.9 0.7 select_reduce_fusion
  10.7 0.5 fusion.2
  11.2 0.5 fusion.1
  11.6 0.2 pad_maximum_fusion
  11.9 2.2 copy.68
  14.1 119.5 %all_to_all.10 = bf16[2,128,2,2048]{3,2,0,1:T(2,128)(2,1)S(1)} all-to-all(bf16[2,128,2,2048]{3,2,0,1:T(2,128)(2,1)S(1)} %copy.68), channel_id=1, replica_groups=mesh['dp'=4,'expert'=128] {'expert'}, dimensions={1} | all-to-all | bytes 4194304 | tf_op jit(solution)/shard_map/all_to_all | solution.py:121
  133.6 3.2 collective-permute-start
  136.8 0.2 convert_bitcast_fusion.1
  137.0 0.3 copy.92
  137.3 1.4 fusion.8
  138.7 3.3 collective-permute-start.1
  142.1 0.2 convert_bitcast_fusion.3
  142.3 0.3 copy.90
  142.6 1.4 fusion.9
  144.0 39.5 %collective-permute-done = bf16[2,128,2,2048]{3,2,0,1:T(2,128)(2,1)} collective-permute-done((bf16[2,128,2,2048]{3,2,0,1:T(2,128)(2,1)S(1)}, bf16[2,128,2,2048]{3,2,0,1:T(2,128)(2,1)}, u32[]{:S(2)}, u32[]{:S(2)}) %collective-permute-start) | collective-permute-done | bytes 2097184 | tf_op jit(solution)/shard_map/ppermute | solution.py:16
  183.5 2.1 collective-permute-start.2
  185.6 1.3 convert_bitcast_fusion.4
  186.9 2.9 copy.88
  189.9 2.8 fusion.10
  192.7 4.6 %broadcast_in_dim.37 = bf16[2,512,2,2048]{3,2,1,0:T(2,128)(2,1)S(1)} broadcast(bf16[]{:T(256)} %constant.46.clone.1), dimensions={} | broadcast | bytes 8388610 | tf_op jit(solution)/shard_map/broadcast_in_dim | solution.py:11
  197.3 1.6 copy_dynamic-update-slice_fusion.3
  198.8 3.2 copy_dynamic-update-slice_fusion.2
  202.0 3.2 copy_dynamic-update-slice_fusion.1
  205.2 27.5 %collective-permute-done.2 = bf16[2,128,2,2048]{3,2,0,1:T(2,128)(2,1)} collective-permute-done((bf16[2,128,2,2048]{3,2,0,1:T(2,128)(2,1)}, bf16[2,128,2,2048]{3,2,0,1:T(2,128)(2,1)}, u32[]{:S(2)}, u32[]{:S(2)}) %collective-permute-start.2) | collective-permute-done | bytes 2097184 | tf_op jit(solution)/shard_map/ppermute | solution.py:16
  232.7 3.2 copy_dynamic-update-slice_fusion
  235.9 7.0 %fusion.34 = (bf16[1,512,2,2048]{3,2,1,0:T(2,128)(2,1)}, bf16[1,512,2,2048]{3,2,1,0:T(2,128)(2,1)}) fusion(bf16[2,512,2,2048]{3,2,1,0:T(2,128)(2,1)S(1)} %copy_dynamic-update-slice_fusion), kind=kLoop, calls=%fused_computation.74 | loop fusion | bytes 16777216 | tf_op jit(solution)/shard_map/slice | solution.py:124
  242.9 7.3 %reshape_squeeze.7 = bf16[1024,2048]{1,0:T(8,128)(2,1)} reshape(bf16[1,512,2,2048]{3,2,1,0:T(2,128)(2,1)} %get-tuple-element.5) | data formatting | bytes 8388608 | tf_op jit(solution)/shard_map/reshape;squeeze | solution.py:123
  250.2 4.8 %fusion.15 = f32[1024,192]{0,1:T(8,128)} fusion(bf16[1024,2048]{1,0:T(8,128)(2,1)} %reshape_squeeze.7, bf16[24,8,16,128]{3,2,1,0:T(8,128)(2,1)S(1)} %bitcast.125), kind=kOutput, calls=%fused_computation.34 | convolution fusion | flops 805306368 | bytes 5767168 | tf_op jit(solution)/shard_map/dot_general | solution.py:56
  254.9 2.4 fusion.18
  257.4 7.3 %reshape_squeeze.6 = bf16[1024,2048]{1,0:T(8,128)(2,1)} reshape(bf16[1,512,2,2048]{3,2,1,0:T(2,128)(2,1)} %get-tuple-element.4) | data formatting | bytes 8388608 | tf_op jit(solution)/shard_map/reshape;squeeze | solution.py:124
  264.7 4.3 multiply_convert_fusion.1
  269.0 0.5 broadcast_in_dim.43
  269.5 1.4 fusion.12
  270.9 0.5 broadcast_in_dim.41
  271.3 0.7 copy-done.6
  272.0 3.4 add_convert_fusion
  275.4 7.7 %reshape.126 = bf16[4,128,2,2048]{3,2,1,0:T(2,128)(2,1)} reshape(bf16[1024,2048]{1,0:T(8,128)(2,1)} %add_convert_fusion) | data formatting | bytes 8388608 | tf_op jit(solution)/shard_map/reshape | solution.py:129
  283.0 6.0 %copy.73 = bf16[4,128,2,2048]{3,1,2,0:T(8,128)(2,1)} copy(bf16[4,128,2,2048]{3,2,1,0:T(2,128)(2,1)} %reshape.126) | data formatting | bytes 8388608 | tf_op jit(solution)/shard_map/reshape | solution.py:129
  289.0 46.9 %reduce-scatter.2.cloned.1.call-done = bf16[1,128,2,2048]{3,1,2,0:T(8,128)(2,1)} async-done(((bf16[4,128,2,2048]{3,1,2,0:T(8,128)(2,1)}), bf16[1,128,2,2048]{3,1,2,0:T(8,128)(2,1)}) %reduce-scatter.2.cloned.1.call-update) | async-done | bytes 1048592 | tf_op jit(solution)/shard_map/reduce_scatter | solution.py:128
  335.9 3.4 copy.74
  339.3 16.7 %all-to-all-start.1 = ((bf16[128,2,2048]{2,1,0:T(2,128)(2,1)}), bf16[128,2,2048]{2,1,0:T(2,128)(2,1)S(1)}, u32[]{:S(2)}, u32[]{:S(2)}) async-start(bf16[128,2,2048]{2,1,0:T(2,128)(2,1)} %copy.74), calls=%async_computation.2 | async-start | bytes 2097152 | tf_op jit(solution)/shard_map/all_to_all | solution.py:134
  356.1 3.5 convolution_convert_fusion.1
  359.5 5.3 %collective-permute-start.5 = (bf16[192,2048]{1,0:T(8,128)(2,1)S(1)}, bf16[192,2048]{1,0:T(8,128)(2,1)S(1)}, u32[]{:S(2)}, u32[]{:S(2)}) collective-permute-start(bf16[192,2048]{1,0:T(8,128)(2,1)S(1)} %convolution_convert_fusion.1), channel_id=1, source_target_pairs={{0,64},{64,0},{1,65},{65,1},{2,66},{66,2},{3,67},{67,3},{4,68},{68... | collective-permute-start | bytes 2359304 | tf_op jit(solution)/shard_map/ppermute | solution.py:35
  364.9 0.6 fusion.32
  366.2 3.3 convolution_convert_fusion.2
  369.5 1.9 collective-permute-start.4
  371.5 1.0 convolution_convert_fusion.3
  372.5 4.9 %collective-permute-start.3 = (bf16[192,2048]{1,0:T(8,128)(2,1)S(1)}, bf16[192,2048]{1,0:T(8,128)(2,1)S(1)}, u32[]{:S(2)}, u32[]{:S(2)}) collective-permute-start(bf16[192,2048]{1,0:T(8,128)(2,1)S(1)} %convolution_convert_fusion.3), channel_id=1, source_target_pairs={{0,64},{64,0},{1,65},{65,1},{2,66},{66,2},{3,67},{67,3},{4,68},{68... | collective-permute-start | bytes 2359304 | tf_op jit(solution)/shard_map/ppermute | solution.py:35
  377.4 9.4 %collective-permute-done.5 = bf16[192,2048]{1,0:T(8,128)(2,1)S(1)} collective-permute-done((bf16[192,2048]{1,0:T(8,128)(2,1)S(1)}, bf16[192,2048]{1,0:T(8,128)(2,1)S(1)}, u32[]{:S(2)}, u32[]{:S(2)}) %collective-permute-start.5) | collective-permute-done | bytes 786464 | tf_op jit(solution)/shard_map/ppermute | solution.py:35
  386.8 1.0 select_bitcast_fusion
  387.7 20.5 %collective-permute-done.4 = bf16[192,2048]{1,0:T(8,128)(2,1)S(1)} collective-permute-done((bf16[192,2048]{1,0:T(8,128)(2,1)S(1)}, bf16[192,2048]{1,0:T(8,128)(2,1)S(1)}, u32[]{:S(2)}, u32[]{:S(2)}) %collective-permute-start.4) | collective-permute-done | bytes 786464 | tf_op jit(solution)/shard_map/ppermute | solution.py:35
  408.2 1.0 select_bitcast_fusion.1
  409.2 16.1 %collective-permute-done.3 = bf16[192,2048]{1,0:T(8,128)(2,1)S(1)} collective-permute-done((bf16[192,2048]{1,0:T(8,128)(2,1)S(1)}, bf16[192,2048]{1,0:T(8,128)(2,1)S(1)}, u32[]{:S(2)}, u32[]{:S(2)}) %collective-permute-start.3) | collective-permute-done | bytes 786464 | tf_op jit(solution)/shard_map/ppermute | solution.py:35
  425.3 1.0 select_bitcast_fusion.2
  426.3 1.3 fusion.3
  (56 shorter events, 0.5 us)
Async XLA Ops:
  7.2 3.5 copy-start
  7.2 4.0 copy-start.11
  7.2 328.7 %reduce-scatter.2.cloned.1.call-start = ((), (), s32[]{:S(2)}) async-start(), calls=%async_computation.3 | async-start | bytes 5242880 | tf_op jit(solution)/shard_map/reduce_scatter | solution.py:128
  14.0 122.7 %copy-start.12 = (f32[1,3,16]{2,0,1:T(1,128)S(1)}, f32[1,3,16]{2,0,1:T(1,128)}, u32[]{:S(2)}) copy-start(f32[1,3,16]{2,0,1:T(1,128)} %param.19) | copy-start | bytes 580
  14.1 122.7 %copy-start.4 = (bf16[1,192,2048]{2,1,0:T(8,128)(2,1)S(1)}, bf16[1,192,2048]{2,1,0:T(8,128)(2,1)}, u32[]{:S(2)}) copy-start(bf16[1,192,2048]{2,1,0:T(8,128)(2,1)} %param.16) | copy-start | bytes 2359300
  133.6 49.9 %collective-permute-start = (bf16[2,128,2,2048]{3,2,0,1:T(2,128)(2,1)S(1)}, bf16[2,128,2,2048]{3,2,0,1:T(2,128)(2,1)}, u32[]{:S(2)}, u32[]{:S(2)}) collective-permute-start(bf16[2,128,2,2048]{3,2,0,1:T(2,128)(2,1)S(1)} %all_to_all.10), channel_id=1, source_target_pairs={{0,128},{128,256},{256,384},{384,0},{1,129},{129,257},{257,385},{3... | collective-permute-start | bytes 6291464 | tf_op jit(solution)/shard_map/ppermute | solution.py:16
  137.0 5.1 %copy-start.5 = (bf16[1,192,2048]{2,1,0:T(8,128)(2,1)S(1)}, bf16[1,192,2048]{2,1,0:T(8,128)(2,1)}, u32[]{:S(2)}) copy-start(bf16[1,192,2048]{2,1,0:T(8,128)(2,1)} %param.17) | copy-start | bytes 2359300
  137.3 4.9 %copy-start.13 = (f32[1,3,16]{2,0,1:T(1,128)S(1)}, f32[1,3,16]{2,0,1:T(1,128)}, u32[]{:S(2)}) copy-start(f32[1,3,16]{2,0,1:T(1,128)} %param.20) | copy-start | bytes 580
  138.7 63.3 %collective-permute-start.1 = (bf16[2,128,2,2048]{3,2,0,1:T(2,128)(2,1)S(1)}, bf16[2,128,2,2048]{3,2,0,1:T(2,128)(2,1)}, u32[]{:S(2)}, u32[]{:S(2)}) collective-permute-start(bf16[2,128,2,2048]{3,2,0,1:T(2,128)(2,1)S(1)} %all_to_all.10), channel_id=1, source_target_pairs={{0,384},{128,0},{256,128},{384,256},{1,385},{129,1},{257,129},{385... | collective-permute-start | bytes 6291464 | tf_op jit(solution)/shard_map/ppermute | solution.py:21
  142.3 43.3 %copy-start.7 = (bf16[1,192,2048]{2,1,0:T(8,128)(2,1)S(1)}, bf16[1,192,2048]{2,1,0:T(8,128)(2,1)}, u32[]{:S(2)}) copy-start(bf16[1,192,2048]{2,1,0:T(8,128)(2,1)} %param.18) | copy-start | bytes 2359300
  183.5 49.2 %collective-permute-start.2 = (bf16[2,128,2,2048]{3,2,0,1:T(2,128)(2,1)}, bf16[2,128,2,2048]{3,2,0,1:T(2,128)(2,1)}, u32[]{:S(2)}, u32[]{:S(2)}) collective-permute-start(bf16[2,128,2,2048]{3,2,0,1:T(2,128)(2,1)} %collective-permute-done), channel_id=1, source_target_pairs={{0,128},{128,256},{256,384},{384,0},{1,129},{129,257},{257,385},{3... | collective-permute-start | bytes 6291464 | tf_op jit(solution)/shard_map/ppermute | solution.py:16
  186.9 2.9 copy-start.14
  242.9 7.3 %copy-start.8 = (bf16[192,16,128]{2,1,0:T(8,128)(2,1)S(1)}, bf16[192,16,128]{2,1,0:T(8,128)(2,1)}, u32[]{:S(2)}) copy-start(bf16[192,16,128]{2,1,0:T(8,128)(2,1)} %fusion.8) | copy-start | bytes 2359300
  250.2 4.8 %copy-start.2 = (bf16[1024,2048]{1,0:T(8,128)(2,1)S(1)}, bf16[1024,2048]{1,0:T(8,128)(2,1)}, u32[]{:S(2)}) copy-start(bf16[1024,2048]{1,0:T(8,128)(2,1)} %reshape_squeeze.7) | copy-start | bytes 12582916
  250.2 4.8 %copy-start.9 = (bf16[192,16,128]{2,1,0:T(8,128)(2,1)S(1)}, bf16[192,16,128]{2,1,0:T(8,128)(2,1)}, u32[]{:S(2)}) copy-start(bf16[192,16,128]{2,1,0:T(8,128)(2,1)} %fusion.9) | copy-start | bytes 2359300
  257.4 7.3 %copy-start.10 = (bf16[192,16,128]{2,1,0:T(8,128)(2,1)S(1)}, bf16[192,16,128]{2,1,0:T(8,128)(2,1)}, u32[]{:S(2)}) copy-start(bf16[192,16,128]{2,1,0:T(8,128)(2,1)} %fusion.10) | copy-start | bytes 2359300
  270.8 1.1 copy-start.6
  335.9 20.1 %copy-start.16 = (f32[1024,192]{0,1:T(8,128)S(1)}, f32[1024,192]{0,1:T(8,128)}, u32[]{:S(2)}) copy-start(f32[1024,192]{0,1:T(8,128)} %fusion.15) | copy-start | bytes 2359300
  339.3 86.9 %all-to-all-start.1 = ((bf16[128,2,2048]{2,1,0:T(2,128)(2,1)}), bf16[128,2,2048]{2,1,0:T(2,128)(2,1)S(1)}, u32[]{:S(2)}, u32[]{:S(2)}) async-start(bf16[128,2,2048]{2,1,0:T(2,128)(2,1)} %copy.74), calls=%async_computation.2 | async-start | bytes 2097152 | tf_op jit(solution)/shard_map/all_to_all | solution.py:134
  356.0 8.8 %copy-start.15 = (s32[128]{0:T(128)S(1)}, s32[128]{0:T(128)}, u32[]{:S(2)}) copy-start(s32[128]{0:T(128)} %param.15) | copy-start | bytes 1540
  359.5 27.3 %collective-permute-start.5 = (bf16[192,2048]{1,0:T(8,128)(2,1)S(1)}, bf16[192,2048]{1,0:T(8,128)(2,1)S(1)}, u32[]{:S(2)}, u32[]{:S(2)}) collective-permute-start(bf16[192,2048]{1,0:T(8,128)(2,1)S(1)} %convolution_convert_fusion.1), channel_id=1, source_target_pairs={{0,64},{64,0},{1,65},{65,1},{2,66},{66,2},{3,67},{67,3},{4,68},{68... | collective-permute-start | bytes 2359304 | tf_op jit(solution)/shard_map/ppermute | solution.py:35
  366.2 5.3 %copy-start.3 = (bf16[1024,2048]{1,0:T(8,128)(2,1)S(1)}, bf16[1024,2048]{1,0:T(8,128)(2,1)}, u32[]{:S(2)}) copy-start(bf16[1024,2048]{1,0:T(8,128)(2,1)} %reshape_squeeze.7) | copy-start | bytes 12582916
  369.5 38.7 %collective-permute-start.4 = (bf16[192,2048]{1,0:T(8,128)(2,1)S(1)}, bf16[192,2048]{1,0:T(8,128)(2,1)S(1)}, u32[]{:S(2)}, u32[]{:S(2)}) collective-permute-start(bf16[192,2048]{1,0:T(8,128)(2,1)S(1)} %convolution_convert_fusion.2), channel_id=1, source_target_pairs={{0,64},{64,0},{1,65},{65,1},{2,66},{66,2},{3,67},{67,3},{4,68},{68... | collective-permute-start | bytes 2359304 | tf_op jit(solution)/shard_map/ppermute | solution.py:35
  372.5 52.8 %collective-permute-start.3 = (bf16[192,2048]{1,0:T(8,128)(2,1)S(1)}, bf16[192,2048]{1,0:T(8,128)(2,1)S(1)}, u32[]{:S(2)}, u32[]{:S(2)}) collective-permute-start(bf16[192,2048]{1,0:T(8,128)(2,1)S(1)} %convolution_convert_fusion.3), channel_id=1, source_target_pairs={{0,64},{64,0},{1,65},{65,1},{2,66},{66,2},{3,67},{67,3},{4,68},{68... | collective-permute-start | bytes 2359304 | tf_op jit(solution)/shard_map/ppermute | solution.py:35
  408.2 19.3 %copy-start.1 = (bf16[24,2048]{1,0:T(8,128)(2,1)S(1)}, bf16[24,2048]{1,0:T(8,128)(2,1)}, u32[]{:S(2)}) copy-start(bf16[24,2048]{1,0:T(8,128)(2,1)} %param.11) | copy-start | bytes 294916
Sparse Core Ops, SparseCore 0:
  289.2 46.6 reduce-scatter.1
